TPU v7x, 32 devices: a whole 2x2x4 slice. The times are simulated.
32 devices in a mesh: groups: 2 (over y), lat: 4 (over x, core), lon: 4 (over z).
Axes of the slice: x: 2, y: 2, z: 4, core: 2. Of those that a mesh axis runs over, the one named last changes fastest.
Arguments:
- tracers: float32 [256, 256, 128], P(('groups', 'lat'), 'lon'), parts along dimension 0, may hold values from 0.3 to 12.6, as said below
- shifts: float32 [4, 3, 16, 32], P('groups'), parts along dimension 0, may hold values from 0 to 1
- diffusivity: float32 [128], P('lat'), may hold values from 0.02 to 0.2, as said below
- source_patch: int32 [4, 16, 32], P('groups'), parts along dimension 0, may hold values from 0 to 511, as said below
Outputs:
- advanced: float32 [256, 256, 128], P(('groups', 'lat'), 'lon'), parts along dimension 0
There are 2 independent parts, one for each index of `groups`. A program takes and returns all parts, laid end to end along the dimension named above; an argument that names none is the same for every part. Nothing has to cross between parts.
Inputs may be any that keep to these rules, and one draw needn't show every extreme that they name: `source_patch`: entry [s, r, c] is the global index of the departure patch of destination patch (r, c) in step s; the departure patch lies in the same tile of 8 patch columns as the destination, and in the same band of 4 patch rows or in one of the two bands on either side. For each step, tile, destination band and other source band, at most 4 destination patches take their departure patch there, and every destination band has a source band that gives exactly 4. `tracers`: positive mixing ratios. `diffusivity`: positive diffusion numbers.
All inputs are finite; a program needn't handle non-finite values.
Results may differ from a plain program's by a relative error of at most 0.0003.
Values sent between devices are 32-bit elements; how exact they have to be, the bound alone decides.
No kernel may reach another device: no remote copies, remote signals or barrier semaphores. Data moves between devices by JAX's collectives and lax.ppermute only.
A program may use at most 64 MiB of HBM per device.

v0:
```python
import math
import jax
import jax.numpy as jnp
from jax import lax
from jax.sharding import PartitionSpec as P

LEV = 4
STEPS = 2
CAP = 4


def from_behind(block, axis, distance):
    devices = range(lax.axis_size(axis))
    route = [(i - distance, i) for i in devices if i - distance in devices]
    return lax.ppermute(block, axis, route)


def extended(cells, sides, width, closed):
    for axis, dim in sides:
        count = lax.axis_size(axis)
        ends = count if closed else count - 1
        head = lax.slice_in_dim(cells, 0, width, axis=dim)
        tail = lax.slice_in_dim(cells, cells.shape[dim] - width, cells.shape[dim], axis=dim)
        cells = jnp.concatenate(
            [
                lax.ppermute(tail, axis, [(i, (i + 1) % count) for i in range(ends)]),
                cells,
                lax.ppermute(head, axis, [((i + 1) % count, i) for i in range(ends)]),
            ],
            axis=dim,
        )
    return cells


def cubic_weights(fraction):
    first_term = -fraction * (fraction - 1.0) * (fraction - 2.0) / 6.0
    second_term = (fraction + 1.0) * (fraction - 1.0) * (fraction - 2.0) / 2.0
    third_term = -(fraction + 1.0) * fraction * (fraction - 2.0) / 2.0
    fourth_term = (fraction + 1.0) * fraction * (fraction - 1.0) / 6.0
    return (first_term, second_term, third_term, fourth_term)


def cubic_matrix(fraction, extent):
    places = jnp.arange(extent)
    running = jnp.zeros(fraction.shape + (extent, extent), jnp.float32)
    for offset, weight in zip(range(-1, 3), cubic_weights(fraction)):
        target_col = jnp.clip(places + offset, 0, extent - 1)
        indicator = (target_col[:, None] == places[None, :]).astype(jnp.float32)
        running = running + weight[..., None, None] * indicator
    return running


def interpolate(patches, fraction_y, fraction_x, fraction_z):
    patch_count = patches.shape[0]
    value_count = patches.shape[2]
    weight_y = cubic_matrix(fraction_y, 8)
    weight_x = cubic_matrix(fraction_x, 8)
    plane_weights = jnp.einsum(
        "nac,nbd->nabcd", weight_y, weight_x, precision=lax.Precision.HIGHEST
    ).reshape(patch_count, 64, 64)
    flat_result = jnp.einsum(
        "nij,njv->niv", plane_weights, patches, precision=lax.Precision.HIGHEST
    )
    stacked = flat_result.reshape(patch_count, 64, LEV, value_count // LEV)
    weight_z = cubic_matrix(fraction_z, LEV)
    levelled = jnp.einsum("nlm,nimt->nilt", weight_z, stacked, precision=lax.Precision.HIGHEST)
    return levelled.reshape(patch_count, 64, value_count)


def to_patches(state_field):
    band_rows = state_field.shape[0] // 8
    band_cols = state_field.shape[1] // 8
    return (
        state_field.reshape(band_rows, 8, band_cols, 8, -1)
        .transpose(0, 2, 1, 3, 4)
        .reshape(band_rows * band_cols, 64, -1)
    )


def from_patches(patches, band_rows, band_cols):
    return (
        patches.reshape(band_rows, band_cols, 8, 8, -1)
        .transpose(0, 2, 1, 3, 4)
        .reshape(band_rows * 8, band_cols * 8, -1)
    )


def column_area(first_row, row_count, total_rows):
    latitude = ((first_row + jnp.arange(row_count)).astype(jnp.float32) + 0.5) * (
        math.pi / total_rows
    ) - 0.5 * math.pi
    return jnp.cos(latitude)


def column_mass(state_field, weights):
    return jnp.sum(weights[:, None, None] * state_field, axis=(0, 1))


def local(tracers, shifts, diffusivity, source_patch):
    lat_count = lax.axis_size("lat")
    lat_index = lax.axis_index("lat")
    lon_index = lax.axis_index("lon")
    row_count, col_count, value_count = tracers.shape
    band_rows = row_count // 8
    band_cols = col_count // 8
    per_device = band_rows * band_cols
    total_cols = source_patch.shape[2]
    band_offsets = (-2, -1, 1, 2)
    weights = column_area(lat_index * row_count, row_count, row_count * lat_count)
    devices = jnp.arange(lat_count)
    slot_range = jnp.arange(CAP)
    state_field = tracers
    target = lax.psum(column_mass(tracers, weights), ("lat", "lon"))
    for step_index in range(STEPS):
        column_ids = lax.dynamic_slice_in_dim(
            source_patch[step_index], lon_index * band_cols, band_cols, 1
        ).reshape(lat_count, per_device)
        fractions = lax.dynamic_slice_in_dim(
            shifts[step_index], lon_index * band_cols, band_cols, 2
        ).reshape(3, lat_count, per_device)
        source_row = column_ids // total_cols
        source_dev = source_row // band_rows
        source_local = (
            source_row % band_rows * band_cols + column_ids % total_cols - lon_index * band_cols
        )
        remote = source_dev != devices[:, None]
        matches = (source_dev[:, :, None] == devices[None, None, :]) & remote[:, :, None]
        slot_ranks = jnp.cumsum(matches.astype(jnp.int32), axis=1) - 1
        slot_of = jnp.sum(jnp.where(matches, slot_ranks, 0), axis=2)
        owned_here = remote & (source_dev == lat_index)
        sending = owned_here[:, :, None] & (slot_of[:, :, None] == slot_range[None, None, :])
        send_local = jnp.sum(jnp.where(sending, source_local[:, :, None], 0), axis=1)
        near_local = jnp.stack(
            [
                lax.dynamic_index_in_dim(send_local, lat_index + offset, 0, keepdims=False)
                for offset in band_offsets
            ]
        )
        own_patches = to_patches(state_field)
        send_patches = own_patches[near_local.reshape(-1)]
        my_dev = lax.dynamic_index_in_dim(source_dev, lat_index, 0, keepdims=False)
        my_slot = lax.dynamic_index_in_dim(slot_of, lat_index, 0, keepdims=False)
        my_local = lax.dynamic_index_in_dim(source_local, lat_index, 0, keepdims=False)
        my_remote = lax.dynamic_index_in_dim(remote, lat_index, 0, keepdims=False)
        my_frac = lax.dynamic_index_in_dim(fractions, lat_index, 1, keepdims=False)
        my_offset = lat_index - my_dev
        pick_index = jnp.where(my_offset < 0, my_offset + 2, my_offset + 1) * CAP + my_slot
        send_frac = jnp.sum(jnp.where(sending[None], fractions[:, :, :, None], 0.0), axis=2)
        near_frac = jnp.stack(
            [
                lax.dynamic_index_in_dim(send_frac, lat_index + offset, 1, keepdims=False)
                for offset in band_offsets
            ],
            axis=1,
        ).reshape(3, -1)
        outgoing = interpolate(send_patches, near_frac[0], near_frac[1], near_frac[2])
        outgoing = outgoing.reshape(4, CAP, 64, value_count)
        arrived = jnp.stack(
            [
                from_behind(outgoing[slot_place], "lat", offset)
                for slot_place, offset in enumerate(band_offsets)
            ]
        )
        arrived = arrived.reshape(4 * CAP, 64, value_count)
        local_done = interpolate(own_patches[my_local], my_frac[0], my_frac[1], my_frac[2])
        finished = jnp.where(my_remote[:, None, None], arrived[pick_index], local_done)
        advected = from_patches(finished, band_rows, band_cols)
        lon_wide = extended(advected, (("lon", 1),), 1, True)
        lat_wide = extended(advected, (("lat", 0),), 1, False)
        laplace = lat_wide[2:] + lat_wide[:-2] + lon_wide[:, 2:] + lon_wide[:, :-2] - 4.0 * advected
        diffused = advected + diffusivity[:, None, None] * laplace
        step_total = lax.psum(column_mass(diffused, weights), ("lat", "lon"))
        state_field = diffused * (target / step_total)[None, None, :]
    return state_field


def solution(mesh):
    return jax.shard_map(
        local,
        mesh=mesh,
        in_specs=(
            P(("groups", "lat"), "lon", None),
            P("groups", None, None, None),
            P("lat"),
            P("groups", None, None),
        ),
        out_specs=P(("groups", "lat"), "lon", None),
        check_vma=False,
    )
```

profile of v0, /device:TPU:0, one launch (start us, length us, event | category | flops | bytes accessed | tf_op | source)
XLA Modules:
  0.0 196.2 jit_solution(16985384277161938453)
XLA Ops:
  9.6 2.9 %fusion.150 = f32[16,64,128]{1,2,0:T(8,128)S(1)} fusion(f32[16,64,64]{2,1,0:T(8,128)} %copy.62, f32[16,64,128]{2,1,0:T(8,128)S(1)} %gather_fusion), kind=kOutput, calls=%fused_computation.360 | convolution fusion | flops 100663296 | bytes 1310720 | tf_op jit(solution)/shard_map/nij,njv->niv/dot_general | solution.py:61
  12.5 2.5 %convolution_bitcast_fusion.1 = f32[16,64,4,32]{1,2,3,0:T(4,128)S(1)} fusion(f32[16,64,4,32]{1,3,2,0:T(8,128)S(1)} %bitcast.153, f32[4,4]{1,0:T(4,128)S(1)} %fusion.111, f32[16]{0:T(128)S(1)} %get-tuple-element.115, f32[4,4]{1,0:T(4,128)S(1)} %fusion.110, f32[16]{0:T(128)S(1)} %get-tuple-element.116, f32[4,4]{1,0:T(4,128)S(1)} %fusion.109, ...), kind=kOutput, calls=%fused_computation.13 | convolution fusion | flops 6293248 | bytes 1049088 | tf_op jit(solution)/shard_map/nlm,nimt->nilt/dot_general | solution.py:66
  19.2 3.7 %collective-permute-start.2 = (f32[4,64,128]{1,2,0:T(8,128)}, f32[4,64,128]{1,2,0:T(8,128)}, u32[]{:S(2)}, u32[]{:S(2)}) collective-permute-start(f32[4,64,128]{1,2,0:T(8,128)} %bitcast.16), channel_id=1, source_target_pairs={{0,4},{4,8},{8,12},{1,5},{5,9},{9,13},{2,6},{6,10},{10,14},{3,7},{... | collective-permute-start | bytes 393224 | tf_op jit(solution)/shard_map/ppermute | solution.py:15
  23.7 6.3 %collective-permute-start.3 = (f32[4,64,128]{1,2,0:T(8,128)}, f32[4,64,128]{1,2,0:T(8,128)}, u32[]{:S(2)}, u32[]{:S(2)}) collective-permute-start(f32[4,64,128]{1,2,0:T(8,128)} %bitcast.18), channel_id=1, source_target_pairs={{0,8},{4,12},{1,9},{5,13},{2,10},{6,14},{3,11},{7,15},{16,24},{20,... | collective-permute-start | bytes 393224 | tf_op jit(solution)/shard_map/ppermute | solution.py:15
  34.1 1.7 copy.70
  41.7 3.5 %fusion.151 = f32[32,64,128]{1,2,0:T(8,128)S(1)} fusion(f32[32,64,64]{2,1,0:T(8,128)S(1)} %copy-done.1, f32[32,64,128]{2,1,0:T(8,128)S(1)} %gather_fusion.2), kind=kOutput, calls=%fused_computation.361 | convolution fusion | flops 201326592 | bytes 2621440 | tf_op jit(solution)/shard_map/nij,njv->niv/dot_general | solution.py:61
  45.2 1.6 broadcast_multiply_fusion
  47.1 5.6 %fusion.4 = f32[32,64,4,32]{1,2,3,0:T(4,128)} fusion(f32[32,64,4,32]{1,3,2,0:T(8,128)S(1)} %bitcast.143, f32[4,4]{1,0:T(4,128)S(1)} %copy-done.10, f32[32]{0:T(128)S(1)} %get-tuple-element.105, f32[4,4]{1,0:T(4,128)S(1)} %copy-done.8, f32[32]{0:T(128)S(1)} %get-tuple-element.106, f32[4,4]{1,0:T(4,128)S(1)} %copy-done.6, f32[32]{0:T(128)S(1)} %get-tuple-element.104, ...), kind=kOutput, calls=%fused_computation.10 | convolution fusion | flops 12586496 | bytes 2097920 | tf_op jit(solution)/shard_map/nlm,nimt->nilt/dot_general | solution.py:66
  53.4 4.8 %copy.73 = f32[32,64,4,32]{3,2,1,0:T(4,128)} copy(f32[32,64,4,32]{1,2,3,0:T(4,128)} %fusion.4) | data formatting | bytes 2097152 | tf_op jit(solution)/shard_map/nlm,nimt->nilt/transpose | solution.py:66
  58.2 4.5 %reshape.1437 = f32[4,8,8,8,128]{4,3,2,1,0:T(8,128)} reshape(f32[32,64,4,32]{3,2,1,0:T(4,128)} %copy.73) | data formatting | bytes 2097152 | tf_op jit(solution)/shard_map/reshape | solution.py:67
  62.9 2.3 %pad_maximum_fusion.8 = f32[4,4,64,128]{2,3,1,0:T(8,128)} fusion(f32[1,4,64,128]{2,3,1,0:T(8,128)} %bitcast.19, f32[1,4,64,128]{2,3,1,0:T(8,128)} %bitcast.17, f32[1,4,64,128]{2,3,1,0:T(8,128)} %bitcast.15, f32[1,4,64,128]{2,3,1,0:T(8,128)} %bitcast.13), kind=kLoop, calls=%fused_computation.34 | loop fusion | flops 393216 | bytes 1048576 | tf_op jit(solution)/shard_map/stack | solution.py:158
  65.2 1.5 copy.69
  66.7 1.6 gather_fusion.1
  68.3 1.7 select_bitcast_fusion.1
  71.5 3.0 %collective-permute-start.5 = (f32[1,64,128]{2,1,0:T(8,128)S(1)}, f32[1,64,128]{2,1,0:T(8,128)S(1)}, u32[]{:S(2)}, u32[]{:S(2)}) collective-permute-start(f32[1,64,128]{2,1,0:T(8,128)S(1)} %get-tuple-element.36), channel_id=1, source_target_pairs={{0,4},{4,8},{8,12},{1,5},{5,9},{9,13},{2,6},{6,10},{10,14},{3,7},{... | collective-permute-start | bytes 98312 | tf_op jit(solution)/shard_map/ppermute | solution.py:26
  74.5 4.8 %collective-permute-start.6 = (f32[32,1,128]{2,1,0:T(1,128)S(1)}, f32[32,1,128]{2,1,0:T(1,128)S(1)}, u32[]{:S(2)}, u32[]{:S(2)}) collective-permute-start(f32[32,1,128]{2,1,0:T(1,128)S(1)} %get-tuple-element.37), channel_id=1, source_target_pairs={{1,0},{2,1},{3,2},{0,3},{5,4},{6,5},{7,6},{4,7},{9,8},{10,9},{11,1... | collective-permute-start | bytes 49160 | tf_op jit(solution)/shard_map/ppermute | solution.py:28
  79.4 3.3 %copy.84 = f32[32,64,64]{2,1,0:T(8,128)} copy(f32[32,64,64]{0,2,1:T(8,128)} %bitcast.142) | data formatting | bytes 1048576 | tf_op jit(solution)/shard_map/reshape | solution.py:60
  84.9 1.9 multiply_reduce_fusion.1
  86.8 30.4 %all-reduce = (f32[128]{0:T(128)S(1)}, f32[128]{0:T(128)S(1)}) all-reduce(f32[128]{0:T(128)S(1)} %get-tuple-element.6, f32[128]{0:T(128)S(1)} %get-tuple-element.5), channel_id=1, replica_groups=mesh['groups'=2,'lat'=4,'lon'=4] {'lat','lon'}, use_global_device_ids=true, to_apply=%region_8.9 | all-reduce | flops 256 | bytes 2048 | tf_op jit(solution)/shard_map/psum | solution.py:113
  119.4 1.8 fusion.152
  121.3 2.5 %convolution_bitcast_fusion = f32[16,64,4,32]{1,2,3,0:T(4,128)S(1)} fusion(f32[16,64,4,32]{1,3,2,0:T(8,128)S(1)} %bitcast.154, f32[16]{0:T(128)S(1)} %copy-done.24, f32[16]{0:T(128)S(1)} %copy-done.25, f32[16]{0:T(128)S(1)} %copy-done.23, f32[16]{0:T(128)S(1)} %copy-done.22, f32[4,4]{1,0:T(4,128)S(1)} %copy-done.10, f32[4,4]{1,0:T(4,128)S(1)} %copy-done.8, ...), kind=kOutput, calls=%fused_computation.12 | convolution fusion | flops 6293248 | bytes 1049088 | tf_op jit(solution)/shard_map/nlm,nimt->nilt/dot_general | solution.py:66
  126.7 3.7 %collective-permute-start.10 = (f32[4,64,128]{1,2,0:T(8,128)S(1)}, f32[4,64,128]{1,2,0:T(8,128)}, u32[]{:S(2)}, u32[]{:S(2)}) collective-permute-start(f32[4,64,128]{1,2,0:T(8,128)S(1)} %bitcast.161), channel_id=1, source_target_pairs={{0,4},{4,8},{8,12},{1,5},{5,9},{9,13},{2,6},{6,10},{10,14},{3,7},{... | collective-permute-start | bytes 393224 | tf_op jit(solution)/shard_map/ppermute | solution.py:15
  130.5 6.3 %collective-permute-start.11 = (f32[4,64,128]{1,2,0:T(8,128)S(1)}, f32[4,64,128]{1,2,0:T(8,128)}, u32[]{:S(2)}, u32[]{:S(2)}) collective-permute-start(f32[4,64,128]{1,2,0:T(8,128)S(1)} %bitcast.162), channel_id=1, source_target_pairs={{0,8},{4,12},{1,9},{5,13},{2,10},{6,14},{3,11},{7,15},{16,24},{20,... | collective-permute-start | bytes 393224 | tf_op jit(solution)/shard_map/ppermute | solution.py:15
  136.8 3.5 %fusion.153 = f32[32,64,128]{1,2,0:T(8,128)S(1)} fusion(f32[32,64,64]{2,1,0:T(8,128)S(1)} %copy-done, f32[32,64,128]{2,1,0:T(8,128)S(1)} %gather_fusion.5), kind=kOutput, calls=%fused_computation.363 | convolution fusion | flops 201326592 | bytes 2621440 | tf_op jit(solution)/shard_map/nij,njv->niv/dot_general | solution.py:61
  140.3 4.5 %fusion.7 = f32[32,64,4,32]{1,2,3,0:T(4,128)S(1)} fusion(f32[32,64,4,32]{1,3,2,0:T(8,128)S(1)} %bitcast.144, f32[32]{0:T(128)S(1)} %copy-done.30, f32[32]{0:T(128)S(1)} %copy-done.31, f32[32]{0:T(128)S(1)} %copy-done.29, f32[32]{0:T(128)S(1)} %copy-done.27, f32[4,4]{1,0:T(4,128)S(1)} %copy-done.10, f32[4,4]{1,0:T(4,128)S(1)} %copy-done.8, ...), kind=kOutput, calls=%fused_computation.11 | convolution fusion | flops 12586496 | bytes 2097920 | tf_op jit(solution)/shard_map/nlm,nimt->nilt/dot_general | solution.py:66
  144.8 3.2 %copy.87 = f32[32,64,4,32]{3,2,1,0:T(4,128)} copy(f32[32,64,4,32]{1,2,3,0:T(4,128)S(1)} %fusion.7) | data formatting | bytes 2097152 | tf_op jit(solution)/shard_map/nlm,nimt->nilt/transpose | solution.py:66
  148.0 3.7 %reshape.1446 = f32[4,8,8,8,128]{4,3,2,1,0:T(8,128)S(1)} reshape(f32[32,64,4,32]{3,2,1,0:T(4,128)} %copy.87) | data formatting | bytes 2097152 | tf_op jit(solution)/shard_map/reshape | solution.py:67
  155.5 3.0 %collective-permute-start.13 = (f32[1,64,128]{2,1,0:T(8,128)S(1)}, f32[1,64,128]{2,1,0:T(8,128)S(1)}, u32[]{:S(2)}, u32[]{:S(2)}) collective-permute-start(f32[1,64,128]{2,1,0:T(8,128)S(1)} %get-tuple-element.28), channel_id=1, source_target_pairs={{0,4},{4,8},{8,12},{1,5},{5,9},{9,13},{2,6},{6,10},{10,14},{3,7},{... | collective-permute-start | bytes 98312 | tf_op jit(solution)/shard_map/ppermute | solution.py:26
  158.7 2.0 %collective-permute-start.15 = (f32[32,1,128]{2,1,0:T(1,128)S(1)}, f32[32,1,128]{2,1,0:T(1,128)S(1)}, u32[]{:S(2)}, u32[]{:S(2)}) collective-permute-start(f32[32,1,128]{2,1,0:T(1,128)S(1)} %get-tuple-element.30), channel_id=1, source_target_pairs={{0,1},{1,2},{2,3},{3,0},{4,5},{5,6},{6,7},{7,4},{8,9},{9,10},{10,1... | collective-permute-start | bytes 49160 | tf_op jit(solution)/shard_map/ppermute | solution.py:26
  160.7 1.7 collective-permute-done.14
  162.4 1.9 collective-permute-done.15
  165.0 29.8 %psum.23 = f32[128]{0:T(128)S(1)} all-reduce(f32[128]{0:T(128)S(1)} %multiply_reduce_fusion), channel_id=1, replica_groups=mesh['groups'=2,'lat'=4,'lon'=4] {'lat','lon'}, use_global_device_ids=true, to_apply=%region_13.14 | all-reduce | flops 128 | bytes 1024 | tf_op jit(solution)/shard_map/psum | solution.py:172
  (212 shorter events, 39.9 us)
Async XLA Ops:
  3.8 8.7 %copy-start.3 = (f32[4,4]{1,0:T(4,128)}, f32[4,4]{1,0:T(4,128)S(1)}, u32[]{:S(2)}) copy-start(f32[4,4]{1,0:T(4,128)S(1)} %fusion.108) | copy-start | bytes 196
  3.9 8.6 %copy-start.5 = (f32[4,4]{1,0:T(4,128)}, f32[4,4]{1,0:T(4,128)S(1)}, u32[]{:S(2)}) copy-start(f32[4,4]{1,0:T(4,128)S(1)} %fusion.109) | copy-start | bytes 196
  3.9 8.6 %copy-start.7 = (f32[4,4]{1,0:T(4,128)}, f32[4,4]{1,0:T(4,128)S(1)}, u32[]{:S(2)}) copy-start(f32[4,4]{1,0:T(4,128)S(1)} %fusion.110) | copy-start | bytes 196
  4.0 8.5 %copy-start.9 = (f32[4,4]{1,0:T(4,128)}, f32[4,4]{1,0:T(4,128)S(1)}, u32[]{:S(2)}) copy-start(f32[4,4]{1,0:T(4,128)S(1)} %fusion.111) | copy-start | bytes 196
  5.4 27.5 %copy-start.11 = (s32[4,32]{1,0:T(4,128)}, s32[4,32]{1,0:T(4,128)S(1)}, u32[]{:S(2)}) copy-start(s32[4,32]{1,0:T(4,128)S(1)} %select_reduce_fusion.3) | copy-start | bytes 1540
  15.0 17.8 %copy-start.21 = (pred[4,32]{1,0:T(4,128)(4,1)S(1)}, pred[4,32]{1,0:T(4,128)(4,1)}, u32[]{:S(2)}) copy-start(pred[4,32]{1,0:T(4,128)(4,1)} %copy-done.20) | copy-start | bytes 388
  15.2 47.7 %collective-permute-start = (f32[4,64,128]{1,2,0:T(8,128)S(1)}, f32[4,64,128]{1,2,0:T(8,128)}, u32[]{:S(2)}, u32[]{:S(2)}) collective-permute-start(f32[4,64,128]{1,2,0:T(8,128)S(1)} %bitcast.158), channel_id=1, source_target_pairs={{8,0},{12,4},{9,1},{13,5},{10,2},{14,6},{11,3},{15,7},{24,16},{28,... | collective-permute-start | bytes 393224 | tf_op jit(solution)/shard_map/ppermute | solution.py:15
  17.2 45.7 %collective-permute-start.1 = (f32[4,64,128]{1,2,0:T(8,128)}, f32[4,64,128]{1,2,0:T(8,128)}, u32[]{:S(2)}, u32[]{:S(2)}) collective-permute-start(f32[4,64,128]{1,2,0:T(8,128)} %bitcast.14), channel_id=1, source_target_pairs={{4,0},{8,4},{12,8},{5,1},{9,5},{13,9},{6,2},{10,6},{14,10},{7,3},{... | collective-permute-start | bytes 393224 | tf_op jit(solution)/shard_map/ppermute | solution.py:15
  19.2 43.6 %collective-permute-start.2 = (f32[4,64,128]{1,2,0:T(8,128)}, f32[4,64,128]{1,2,0:T(8,128)}, u32[]{:S(2)}, u32[]{:S(2)}) collective-permute-start(f32[4,64,128]{1,2,0:T(8,128)} %bitcast.16), channel_id=1, source_target_pairs={{0,4},{4,8},{8,12},{1,5},{5,9},{9,13},{2,6},{6,10},{10,14},{3,7},{... | collective-permute-start | bytes 393224 | tf_op jit(solution)/shard_map/ppermute | solution.py:15
  23.7 39.2 %collective-permute-start.3 = (f32[4,64,128]{1,2,0:T(8,128)}, f32[4,64,128]{1,2,0:T(8,128)}, u32[]{:S(2)}, u32[]{:S(2)}) collective-permute-start(f32[4,64,128]{1,2,0:T(8,128)} %bitcast.18), channel_id=1, source_target_pairs={{0,8},{4,12},{1,9},{5,13},{2,10},{6,14},{3,11},{7,15},{16,24},{20,... | collective-permute-start | bytes 393224 | tf_op jit(solution)/shard_map/ppermute | solution.py:15
  34.1 6.2 %copy-start.13 = (s32[4,4]{1,0:T(4,128)S(1)}, s32[4,4]{1,0:T(4,128)}, u32[]{:S(2)}) copy-start(s32[4,4]{1,0:T(4,128)} %select_reduce_fusion) | copy-start | bytes 196
  34.1 6.9 %copy-start.14 = (f32[1,4,4]{2,1,0:T(4,128)S(1)}, f32[1,4,4]{2,1,0:T(4,128)}, u32[]{:S(2)}) copy-start(f32[1,4,4]{2,1,0:T(4,128)} %get-tuple-element.57) | copy-start | bytes 196
  35.8 5.8 %copy-start.1 = (f32[32,64,64]{2,1,0:T(8,128)S(1)}, f32[32,64,64]{2,1,0:T(8,128)}, u32[]{:S(2)}) copy-start(f32[32,64,64]{2,1,0:T(8,128)} %copy.70) | copy-start | bytes 1572868
  47.1 6.3 %copy-start.19 = (pred[4,32]{1,0:T(4,128)(4,1)S(1)}, pred[4,32]{1,0:T(4,128)(4,1)}, u32[]{:S(2)}) copy-start(pred[4,32]{1,0:T(4,128)(4,1)} %copy-done.18) | copy-start | bytes 388
  68.3 11.1 %copy-start.17 = (pred[4,32]{1,0:T(4,128)(4,1)S(1)}, pred[4,32]{1,0:T(4,128)(4,1)}, u32[]{:S(2)}) copy-start(pred[4,32]{1,0:T(4,128)(4,1)} %copy-done.16) | copy-start | bytes 388
  70.2 14.7 %collective-permute-start.4 = (f32[1,64,128]{2,1,0:T(8,128)S(1)}, f32[1,64,128]{2,1,0:T(8,128)S(1)}, u32[]{:S(2)}, u32[]{:S(2)}) collective-permute-start(f32[1,64,128]{2,1,0:T(8,128)S(1)} %get-tuple-element.35), channel_id=1, source_target_pairs={{4,0},{8,4},{12,8},{5,1},{9,5},{13,9},{6,2},{10,6},{14,10},{7,3},{... | collective-permute-start | bytes 98312 | tf_op jit(solution)/shard_map/ppermute | solution.py:28
  71.5 13.4 %collective-permute-start.5 = (f32[1,64,128]{2,1,0:T(8,128)S(1)}, f32[1,64,128]{2,1,0:T(8,128)S(1)}, u32[]{:S(2)}, u32[]{:S(2)}) collective-permute-start(f32[1,64,128]{2,1,0:T(8,128)S(1)} %get-tuple-element.36), channel_id=1, source_target_pairs={{0,4},{4,8},{8,12},{1,5},{5,9},{9,13},{2,6},{6,10},{10,14},{3,7},{... | collective-permute-start | bytes 98312 | tf_op jit(solution)/shard_map/ppermute | solution.py:26
  74.5 9.7 %collective-permute-start.6 = (f32[32,1,128]{2,1,0:T(1,128)S(1)}, f32[32,1,128]{2,1,0:T(1,128)S(1)}, u32[]{:S(2)}, u32[]{:S(2)}) collective-permute-start(f32[32,1,128]{2,1,0:T(1,128)S(1)} %get-tuple-element.37), channel_id=1, source_target_pairs={{1,0},{2,1},{3,2},{0,3},{5,4},{6,5},{7,6},{4,7},{9,8},{10,9},{11,1... | collective-permute-start | bytes 49160 | tf_op jit(solution)/shard_map/ppermute | solution.py:28
  79.3 5.5 %collective-permute-start.7 = (f32[32,1,128]{2,1,0:T(1,128)S(1)}, f32[32,1,128]{2,1,0:T(1,128)S(1)}, u32[]{:S(2)}, u32[]{:S(2)}) collective-permute-start(f32[32,1,128]{2,1,0:T(1,128)S(1)} %get-tuple-element.38), channel_id=1, source_target_pairs={{0,1},{1,2},{2,3},{3,0},{4,5},{5,6},{6,7},{7,4},{8,9},{9,10},{10,1... | collective-permute-start | bytes 49160 | tf_op jit(solution)/shard_map/ppermute | solution.py:26
  123.8 13.0 %copy-start = (f32[32,64,64]{2,1,0:T(8,128)S(1)}, f32[32,64,64]{2,1,0:T(8,128)}, u32[]{:S(2)}) copy-start(f32[32,64,64]{2,1,0:T(8,128)} %copy.84) | copy-start | bytes 1572868
  123.9 27.8 %collective-permute-start.8 = (f32[4,64,128]{1,2,0:T(8,128)S(1)}, f32[4,64,128]{1,2,0:T(8,128)S(1)}, u32[]{:S(2)}, u32[]{:S(2)}) collective-permute-start(f32[4,64,128]{1,2,0:T(8,128)S(1)} %bitcast.159), channel_id=1, source_target_pairs={{8,0},{12,4},{9,1},{13,5},{10,2},{14,6},{11,3},{15,7},{24,16},{28,... | collective-permute-start | bytes 393224 | tf_op jit(solution)/shard_map/ppermute | solution.py:15
  125.4 26.4 %collective-permute-start.9 = (f32[4,64,128]{1,2,0:T(8,128)S(1)}, f32[4,64,128]{1,2,0:T(8,128)}, u32[]{:S(2)}, u32[]{:S(2)}) collective-permute-start(f32[4,64,128]{1,2,0:T(8,128)S(1)} %bitcast.160), channel_id=1, source_target_pairs={{4,0},{8,4},{12,8},{5,1},{9,5},{13,9},{6,2},{10,6},{14,10},{7,3},{... | collective-permute-start | bytes 393224 | tf_op jit(solution)/shard_map/ppermute | solution.py:15
  126.7 25.0 %collective-permute-start.10 = (f32[4,64,128]{1,2,0:T(8,128)S(1)}, f32[4,64,128]{1,2,0:T(8,128)}, u32[]{:S(2)}, u32[]{:S(2)}) collective-permute-start(f32[4,64,128]{1,2,0:T(8,128)S(1)} %bitcast.161), channel_id=1, source_target_pairs={{0,4},{4,8},{8,12},{1,5},{5,9},{9,13},{2,6},{6,10},{10,14},{3,7},{... | collective-permute-start | bytes 393224 | tf_op jit(solution)/shard_map/ppermute | solution.py:15
  130.5 9.8 %copy-start.27 = (f32[32]{0:T(128)S(1)}, f32[32]{0:T(128)}, u32[]{:S(2)}) copy-start(f32[32]{0:T(128)} %get-tuple-element.9) | copy-start | bytes 388
  130.5 9.8 %copy-start.29 = (f32[32]{0:T(128)S(1)}, f32[32]{0:T(128)}, u32[]{:S(2)}) copy-start(f32[32]{0:T(128)} %get-tuple-element.83) | copy-start | bytes 388
  130.5 9.8 %copy-start.30 = (f32[32]{0:T(128)S(1)}, f32[32]{0:T(128)}, u32[]{:S(2)}) copy-start(f32[32]{0:T(128)} %get-tuple-element.84) | copy-start | bytes 388
  130.5 9.8 %copy-start.31 = (f32[32]{0:T(128)S(1)}, f32[32]{0:T(128)}, u32[]{:S(2)}) copy-start(f32[32]{0:T(128)} %get-tuple-element.85) | copy-start | bytes 388
  130.5 21.2 %collective-permute-start.11 = (f32[4,64,128]{1,2,0:T(8,128)S(1)}, f32[4,64,128]{1,2,0:T(8,128)}, u32[]{:S(2)}, u32[]{:S(2)}) collective-permute-start(f32[4,64,128]{1,2,0:T(8,128)S(1)} %bitcast.162), channel_id=1, source_target_pairs={{0,8},{4,12},{1,9},{5,13},{2,10},{6,14},{3,11},{7,15},{16,24},{20,... | collective-permute-start | bytes 393224 | tf_op jit(solution)/shard_map/ppermute | solution.py:15
  154.2 10.0 %collective-permute-start.12 = (f32[1,64,128]{2,1,0:T(8,128)S(1)}, f32[1,64,128]{2,1,0:T(8,128)S(1)}, u32[]{:S(2)}, u32[]{:S(2)}) collective-permute-start(f32[1,64,128]{2,1,0:T(8,128)S(1)} %get-tuple-element.27), channel_id=1, source_target_pairs={{4,0},{8,4},{12,8},{5,1},{9,5},{13,9},{6,2},{10,6},{14,10},{7,3},{... | collective-permute-start | bytes 98312 | tf_op jit(solution)/shard_map/ppermute | solution.py:28
  155.5 8.7 %collective-permute-start.13 = (f32[1,64,128]{2,1,0:T(8,128)S(1)}, f32[1,64,128]{2,1,0:T(8,128)S(1)}, u32[]{:S(2)}, u32[]{:S(2)}) collective-permute-start(f32[1,64,128]{2,1,0:T(8,128)S(1)} %get-tuple-element.28), channel_id=1, source_target_pairs={{0,4},{4,8},{8,12},{1,5},{5,9},{9,13},{2,6},{6,10},{10,14},{3,7},{... | collective-permute-start | bytes 98312 | tf_op jit(solution)/shard_map/ppermute | solution.py:26
  158.6 3.8 %collective-permute-start.14 = (f32[32,1,128]{2,1,0:T(1,128)S(1)}, f32[32,1,128]{2,1,0:T(1,128)S(1)}, u32[]{:S(2)}, u32[]{:S(2)}) collective-permute-start(f32[32,1,128]{2,1,0:T(1,128)S(1)} %get-tuple-element.29), channel_id=1, source_target_pairs={{1,0},{2,1},{3,2},{0,3},{5,4},{6,5},{7,6},{4,7},{9,8},{10,9},{11,1... | collective-permute-start | bytes 49160 | tf_op jit(solution)/shard_map/ppermute | solution.py:28
  158.7 5.6 %collective-permute-start.15 = (f32[32,1,128]{2,1,0:T(1,128)S(1)}, f32[32,1,128]{2,1,0:T(1,128)S(1)}, u32[]{:S(2)}, u32[]{:S(2)}) collective-permute-start(f32[32,1,128]{2,1,0:T(1,128)S(1)} %get-tuple-element.30), channel_id=1, source_target_pairs={{0,1},{1,2},{2,3},{3,0},{4,5},{5,6},{6,7},{7,4},{8,9},{9,10},{10,1... | collective-permute-start | bytes 49160 | tf_op jit(solution)/shard_map/ppermute | solution.py:26
  (16 other events, 35.7 us)
where the time goes:
time: 197 us; the launch traced here: 196 us
  blocking collectives  60.2 us (31%)
  starting transfers between devices  40.9 us (21%)
  local copies, waits for them, and re-layouts  39.2 us (20%)
  matrix products  26.7 us (14%)
  other arithmetic  24.1 us (12%)
  waiting for transfers between devices  4.2 us (2%)
    psum x1, blocking collectives, local(): target = lax.psum(column_mass(tracers, weights), ('lat', 'lon'))  30.4 us
    psum x1, blocking collectives, local(): step_total = lax.psum(column_mass(diffused, weights), ('lat', 'lon'))  29.8 us
    ppermute x8, starting transfers between devices, from_behind(): return lax.ppermute(block, axis, route)  25.3 us
    dot_general x4, matrix products, interpolate(): jnp.einsum('nlm,nimt->nilt', weight_z, stacked, precision=lax.Precision.H...  15.1 us
    dot_general x4, matrix products, interpolate(): jnp.einsum('nij,njv->niv', plane_weights, patches, precision=lax.Precisio...  11.6 us
    reshape x2, local copies, waits for them, and re-layouts, interpolate(): return levelled.reshape(patch_count, 64, value_count)  8.25 us
    ppermute x4, starting transfers between devices, extended(): lax.ppermute(tail, axis, [(i, (i + 1) % count) for i in range(ends)])  8.08 us
    transpose x2, local copies, waits for them, and re-layouts, interpolate(): jnp.einsum('nlm,nimt->nilt', weight_z, stacked, precision=lax.Precision.H...  8.02 us
  transfers between devices with their start and end apart: 16, of which 3 were waited for; matrix products, arithmetic and copies ran while one was open for 28% of the time, Pallas kernels for 0%

commit v1 on v0

--- a/solution.py
+++ b/solution.py
@@ -7,6 +7,11 @@
 LEV = 4
 STEPS = 2
 CAP = 4
+
+
+def by_each_axis(array, one, other):
+    partial = lax.psum(array, one)
+    return lax.psum(partial, other)
 
 
 def from_behind(block, axis, distance):
@@ -169,7 +174,7 @@
         lat_wide = extended(advected, (("lat", 0),), 1, False)
         laplace = lat_wide[2:] + lat_wide[:-2] + lon_wide[:, 2:] + lon_wide[:, :-2] - 4.0 * advected
         diffused = advected + diffusivity[:, None, None] * laplace
-        step_total = lax.psum(column_mass(diffused, weights), ("lat", "lon"))
+        step_total = by_each_axis(column_mass(diffused, weights), "lon", "lat")
         state_field = diffused * (target / step_total)[None, None, :]
     return state_field
 

time: 197 us -> 199 us (1.010)
    psum x1 -> x4, blocking collectives: 29.8 us -> 31.9 us  [the longest x2 20.4 us: by_each_axis(): partial = lax.psum(array, one)]
where the time goes in v1:
time: 199 us; the launch traced here: 198 us
  blocking collectives  61.5 us (31%)
  starting transfers between devices  40.2 us (20%)
  local copies, waits for them, and re-layouts  39.2 us (20%)
  matrix products  26.6 us (13%)
  other arithmetic  24 us (12%)
  waiting for transfers between devices  5.09 us (3%)
    psum x1, blocking collectives, local(): target = lax.psum(column_mass(tracers, weights), ('lat', 'lon'))  29.7 us
    ppermute x8, starting transfers between devices, from_behind(): return lax.ppermute(block, axis, route)  24.3 us
    psum x2, blocking collectives, by_each_axis(): partial = lax.psum(array, one)  20.4 us
    dot_general x4, matrix products, interpolate(): jnp.einsum('nlm,nimt->nilt', weight_z, stacked, precision=lax.Precision.H...  15.1 us
    dot_general x4, matrix products, interpolate(): jnp.einsum('nij,njv->niv', plane_weights, patches, precision=lax.Precisio...  11.6 us
    psum x2, blocking collectives, by_each_axis(): return lax.psum(partial, other)  11.5 us
    ppermute x4, starting transfers between devices, extended(): lax.ppermute(head, axis, [((i + 1) % count, i) for i in range(ends)])  8.71 us
    reshape x2, local copies, waits for them, and re-layouts, interpolate(): return levelled.reshape(patch_count, 64, value_count)  8.24 us
  transfers between devices with their start and end apart: 16, of which 3 were waited for; matrix products, arithmetic and copies ran while one was open for 28% of the time, Pallas kernels for 0%

profile of v1, /device:TPU:0, one launch (start us, length us, event | category | flops | bytes accessed | tf_op | source)
XLA Modules:
  0.0 197.6 jit_solution(4569870054052340208)
XLA Ops:
  9.6 2.9 %fusion.150 = f32[16,64,128]{1,2,0:T(8,128)S(1)} fusion(f32[16,64,64]{2,1,0:T(8,128)} %copy.62, f32[16,64,128]{2,1,0:T(8,128)S(1)} %gather_fusion), kind=kOutput, calls=%fused_computation.360 | convolution fusion | flops 100663296 | bytes 1310720 | tf_op jit(solution)/shard_map/nij,njv->niv/dot_general | solution.py:66
  12.5 2.5 %convolution_bitcast_fusion.1 = f32[16,64,4,32]{1,2,3,0:T(4,128)S(1)} fusion(f32[16,64,4,32]{1,3,2,0:T(8,128)S(1)} %bitcast.153, f32[4,4]{1,0:T(4,128)S(1)} %fusion.111, f32[16]{0:T(128)S(1)} %get-tuple-element.113, f32[4,4]{1,0:T(4,128)S(1)} %fusion.110, f32[16]{0:T(128)S(1)} %get-tuple-element.114, f32[4,4]{1,0:T(4,128)S(1)} %fusion.109, ...), kind=kOutput, calls=%fused_computation.13 | convolution fusion | flops 6293248 | bytes 1049088 | tf_op jit(solution)/shard_map/nlm,nimt->nilt/dot_general | solution.py:71
  19.2 3.7 %collective-permute-start.2 = (f32[4,64,128]{1,2,0:T(8,128)}, f32[4,64,128]{1,2,0:T(8,128)}, u32[]{:S(2)}, u32[]{:S(2)}) collective-permute-start(f32[4,64,128]{1,2,0:T(8,128)} %bitcast.16), channel_id=1, source_target_pairs={{0,4},{4,8},{8,12},{1,5},{5,9},{9,13},{2,6},{6,10},{10,14},{3,7},{... | collective-permute-start | bytes 393224 | tf_op jit(solution)/shard_map/ppermute | solution.py:20
  23.7 6.3 %collective-permute-start.3 = (f32[4,64,128]{1,2,0:T(8,128)}, f32[4,64,128]{1,2,0:T(8,128)}, u32[]{:S(2)}, u32[]{:S(2)}) collective-permute-start(f32[4,64,128]{1,2,0:T(8,128)} %bitcast.18), channel_id=1, source_target_pairs={{0,8},{4,12},{1,9},{5,13},{2,10},{6,14},{3,11},{7,15},{16,24},{20,... | collective-permute-start | bytes 393224 | tf_op jit(solution)/shard_map/ppermute | solution.py:20
  34.0 1.7 copy.70
  41.6 3.5 %fusion.151 = f32[32,64,128]{1,2,0:T(8,128)S(1)} fusion(f32[32,64,64]{2,1,0:T(8,128)S(1)} %copy-done.1, f32[32,64,128]{2,1,0:T(8,128)S(1)} %gather_fusion.2), kind=kOutput, calls=%fused_computation.361 | convolution fusion | flops 201326592 | bytes 2621440 | tf_op jit(solution)/shard_map/nij,njv->niv/dot_general | solution.py:66
  45.1 1.6 broadcast_multiply_fusion
  47.1 5.5 %fusion.4 = f32[32,64,4,32]{1,2,3,0:T(4,128)} fusion(f32[32,64,4,32]{1,3,2,0:T(8,128)S(1)} %bitcast.143, f32[4,4]{1,0:T(4,128)S(1)} %copy-done.10, f32[32]{0:T(128)S(1)} %get-tuple-element.103, f32[4,4]{1,0:T(4,128)S(1)} %copy-done.8, f32[32]{0:T(128)S(1)} %get-tuple-element.104, f32[4,4]{1,0:T(4,128)S(1)} %copy-done.6, f32[32]{0:T(128)S(1)} %get-tuple-element.102, ...), kind=kOutput, calls=%fused_computation.10 | convolution fusion | flops 12586496 | bytes 2097920 | tf_op jit(solution)/shard_map/nlm,nimt->nilt/dot_general | solution.py:71
  53.3 4.8 %copy.73 = f32[32,64,4,32]{3,2,1,0:T(4,128)} copy(f32[32,64,4,32]{1,2,3,0:T(4,128)} %fusion.4) | data formatting | bytes 2097152 | tf_op jit(solution)/shard_map/nlm,nimt->nilt/transpose | solution.py:71
  58.1 4.5 %reshape.1437 = f32[4,8,8,8,128]{4,3,2,1,0:T(8,128)} reshape(f32[32,64,4,32]{3,2,1,0:T(4,128)} %copy.73) | data formatting | bytes 2097152 | tf_op jit(solution)/shard_map/reshape | solution.py:72
  62.8 2.3 %pad_maximum_fusion.8 = f32[4,4,64,128]{2,3,1,0:T(8,128)} fusion(f32[1,4,64,128]{2,3,1,0:T(8,128)} %bitcast.19, f32[1,4,64,128]{2,3,1,0:T(8,128)} %bitcast.17, f32[1,4,64,128]{2,3,1,0:T(8,128)} %bitcast.15, f32[1,4,64,128]{2,3,1,0:T(8,128)} %bitcast.13), kind=kLoop, calls=%fused_computation.34 | loop fusion | flops 393216 | bytes 1048576 | tf_op jit(solution)/shard_map/stack | solution.py:163
  68.2 1.7 select_bitcast_fusion.1
  71.4 3.0 %collective-permute-start.5 = (f32[1,64,128]{2,1,0:T(8,128)S(1)}, f32[1,64,128]{2,1,0:T(8,128)S(1)}, u32[]{:S(2)}, u32[]{:S(2)}) collective-permute-start(f32[1,64,128]{2,1,0:T(8,128)S(1)} %get-tuple-element.34), channel_id=1, source_target_pairs={{0,4},{4,8},{8,12},{1,5},{5,9},{9,13},{2,6},{6,10},{10,14},{3,7},{... | collective-permute-start | bytes 98312 | tf_op jit(solution)/shard_map/ppermute | solution.py:31
  74.4 4.8 %collective-permute-start.6 = (f32[32,1,128]{2,1,0:T(1,128)S(1)}, f32[32,1,128]{2,1,0:T(1,128)S(1)}, u32[]{:S(2)}, u32[]{:S(2)}) collective-permute-start(f32[32,1,128]{2,1,0:T(1,128)S(1)} %get-tuple-element.35), channel_id=1, source_target_pairs={{1,0},{2,1},{3,2},{0,3},{5,4},{6,5},{7,6},{4,7},{9,8},{10,9},{11,1... | collective-permute-start | bytes 49160 | tf_op jit(solution)/shard_map/ppermute | solution.py:33
  79.3 3.3 %copy.84 = f32[32,64,64]{2,1,0:T(8,128)} copy(f32[32,64,64]{0,2,1:T(8,128)} %bitcast.142) | data formatting | bytes 1048576 | tf_op jit(solution)/shard_map/reshape | solution.py:65
  84.8 1.9 multiply_reduce_fusion.1
  86.7 11.9 %psum.36 = f32[128]{0:T(128)S(1)} all-reduce(f32[128]{0:T(128)S(1)} %get-tuple-element.5), channel_id=1, replica_groups=mesh['groups'=2,'lat'=4,'lon'=4] {'lon'}, use_global_device_ids=true, to_apply=%region_10.11 | all-reduce | flops 128 | bytes 1024 | tf_op jit(solution)/shard_map/psum | solution.py:13
  98.5 5.7 %psum.37 = f32[128]{0:T(128)S(1)} all-reduce(f32[128]{0:T(128)S(1)} %psum.36), channel_id=1, replica_groups=mesh['groups'=2,'lat'=4,'lon'=4] {'lat'}, use_global_device_ids=true, to_apply=%region_11.12 | all-reduce | flops 128 | bytes 1024 | tf_op jit(solution)/shard_map/psum | solution.py:14
  104.3 29.7 %psum.35 = f32[128]{0:T(128)S(1)} all-reduce(f32[128]{0:T(128)S(1)} %get-tuple-element.6), channel_id=1, replica_groups=mesh['groups'=2,'lat'=4,'lon'=4] {'lat','lon'}, use_global_device_ids=true, to_apply=%region_8.9 | all-reduce | flops 128 | bytes 1024 | tf_op jit(solution)/shard_map/psum | solution.py:118
  136.2 1.8 fusion.152
  138.1 2.5 %convolution_bitcast_fusion = f32[16,64,4,32]{1,2,3,0:T(4,128)S(1)} fusion(f32[16,64,4,32]{1,3,2,0:T(8,128)S(1)} %bitcast.154, f32[16]{0:T(128)S(1)} %copy-done.24, f32[16]{0:T(128)S(1)} %copy-done.25, f32[16]{0:T(128)S(1)} %copy-done.23, f32[16]{0:T(128)S(1)} %copy-done.22, f32[4,4]{1,0:T(4,128)S(1)} %copy-done.10, f32[4,4]{1,0:T(4,128)S(1)} %copy-done.8, ...), kind=kOutput, calls=%fused_computation.12 | convolution fusion | flops 6293248 | bytes 1049088 | tf_op jit(solution)/shard_map/nlm,nimt->nilt/dot_general | solution.py:71
  143.5 3.8 %collective-permute-start.10 = (f32[4,64,128]{1,2,0:T(8,128)S(1)}, f32[4,64,128]{1,2,0:T(8,128)}, u32[]{:S(2)}, u32[]{:S(2)}) collective-permute-start(f32[4,64,128]{1,2,0:T(8,128)S(1)} %bitcast.161), channel_id=1, source_target_pairs={{0,4},{4,8},{8,12},{1,5},{5,9},{9,13},{2,6},{6,10},{10,14},{3,7},{... | collective-permute-start | bytes 393224 | tf_op jit(solution)/shard_map/ppermute | solution.py:20
  147.3 5.3 %collective-permute-start.11 = (f32[4,64,128]{1,2,0:T(8,128)S(1)}, f32[4,64,128]{1,2,0:T(8,128)}, u32[]{:S(2)}, u32[]{:S(2)}) collective-permute-start(f32[4,64,128]{1,2,0:T(8,128)S(1)} %bitcast.162), channel_id=1, source_target_pairs={{0,8},{4,12},{1,9},{5,13},{2,10},{6,14},{3,11},{7,15},{16,24},{20,... | collective-permute-start | bytes 393224 | tf_op jit(solution)/shard_map/ppermute | solution.py:20
  152.6 3.5 %fusion.153 = f32[32,64,128]{1,2,0:T(8,128)S(1)} fusion(f32[32,64,64]{2,1,0:T(8,128)S(1)} %copy-done, f32[32,64,128]{2,1,0:T(8,128)S(1)} %gather_fusion.5), kind=kOutput, calls=%fused_computation.363 | convolution fusion | flops 201326592 | bytes 2621440 | tf_op jit(solution)/shard_map/nij,njv->niv/dot_general | solution.py:66
  156.1 4.5 %fusion.7 = f32[32,64,4,32]{1,2,3,0:T(4,128)S(1)} fusion(f32[32,64,4,32]{1,3,2,0:T(8,128)S(1)} %bitcast.144, f32[32]{0:T(128)S(1)} %copy-done.30, f32[32]{0:T(128)S(1)} %copy-done.31, f32[32]{0:T(128)S(1)} %copy-done.29, f32[32]{0:T(128)S(1)} %copy-done.27, f32[4,4]{1,0:T(4,128)S(1)} %copy-done.10, f32[4,4]{1,0:T(4,128)S(1)} %copy-done.8, ...), kind=kOutput, calls=%fused_computation.11 | convolution fusion | flops 12586496 | bytes 2097920 | tf_op jit(solution)/shard_map/nlm,nimt->nilt/dot_general | solution.py:71
  160.6 3.2 %copy.87 = f32[32,64,4,32]{3,2,1,0:T(4,128)} copy(f32[32,64,4,32]{1,2,3,0:T(4,128)S(1)} %fusion.7) | data formatting | bytes 2097152 | tf_op jit(solution)/shard_map/nlm,nimt->nilt/transpose | solution.py:71
  163.8 3.7 %reshape.1446 = f32[4,8,8,8,128]{4,3,2,1,0:T(8,128)S(1)} reshape(f32[32,64,4,32]{3,2,1,0:T(4,128)} %copy.87) | data formatting | bytes 2097152 | tf_op jit(solution)/shard_map/reshape | solution.py:72
  171.3 3.0 %collective-permute-start.13 = (f32[1,64,128]{2,1,0:T(8,128)S(1)}, f32[1,64,128]{2,1,0:T(8,128)S(1)}, u32[]{:S(2)}, u32[]{:S(2)}) collective-permute-start(f32[1,64,128]{2,1,0:T(8,128)S(1)} %get-tuple-element.26), channel_id=1, source_target_pairs={{0,4},{4,8},{8,12},{1,5},{5,9},{9,13},{2,6},{6,10},{10,14},{3,7},{... | collective-permute-start | bytes 98312 | tf_op jit(solution)/shard_map/ppermute | solution.py:31
  176.7 1.7 collective-permute-done.14
  178.4 2.8 %collective-permute-done.15 = f32[32,1,128]{2,1,0:T(1,128)S(1)} collective-permute-done((f32[32,1,128]{2,1,0:T(1,128)S(1)}, f32[32,1,128]{2,1,0:T(1,128)S(1)}, u32[]{:S(2)}, u32[]{:S(2)}) %collective-permute-start.15) | collective-permute-done | bytes 16416 | tf_op jit(solution)/shard_map/ppermute | solution.py:31
  181.9 8.5 %psum.38 = f32[128]{0:T(128)S(1)} all-reduce(f32[128]{0:T(128)S(1)} %multiply_reduce_fusion), channel_id=1, replica_groups=mesh['groups'=2,'lat'=4,'lon'=4] {'lon'}, use_global_device_ids=true, to_apply=%region_14.15 | all-reduce | flops 128 | bytes 1024 | tf_op jit(solution)/shard_map/psum | solution.py:13
  190.5 5.7 %psum.39 = f32[128]{0:T(128)S(1)} all-reduce(f32[128]{0:T(128)S(1)} %psum.38), channel_id=1, replica_groups=mesh['groups'=2,'lat'=4,'lon'=4] {'lat'}, use_global_device_ids=true, to_apply=%region_15.16 | all-reduce | flops 128 | bytes 1024 | tf_op jit(solution)/shard_map/psum | solution.py:14
  (215 shorter events, 45.2 us)
Async XLA Ops:
  3.8 8.7 %copy-start.3 = (f32[4,4]{1,0:T(4,128)}, f32[4,4]{1,0:T(4,128)S(1)}, u32[]{:S(2)}) copy-start(f32[4,4]{1,0:T(4,128)S(1)} %fusion.108) | copy-start | bytes 196
  3.9 8.6 %copy-start.5 = (f32[4,4]{1,0:T(4,128)}, f32[4,4]{1,0:T(4,128)S(1)}, u32[]{:S(2)}) copy-start(f32[4,4]{1,0:T(4,128)S(1)} %fusion.109) | copy-start | bytes 196
  3.9 8.5 %copy-start.7 = (f32[4,4]{1,0:T(4,128)}, f32[4,4]{1,0:T(4,128)S(1)}, u32[]{:S(2)}) copy-start(f32[4,4]{1,0:T(4,128)S(1)} %fusion.110) | copy-start | bytes 196
  4.0 8.5 %copy-start.9 = (f32[4,4]{1,0:T(4,128)}, f32[4,4]{1,0:T(4,128)S(1)}, u32[]{:S(2)}) copy-start(f32[4,4]{1,0:T(4,128)S(1)} %fusion.111) | copy-start | bytes 196
  5.4 27.4 %copy-start.11 = (s32[4,32]{1,0:T(4,128)}, s32[4,32]{1,0:T(4,128)S(1)}, u32[]{:S(2)}) copy-start(s32[4,32]{1,0:T(4,128)S(1)} %select_reduce_fusion.3) | copy-start | bytes 1540
  15.0 17.7 %copy-start.21 = (pred[4,32]{1,0:T(4,128)(4,1)S(1)}, pred[4,32]{1,0:T(4,128)(4,1)}, u32[]{:S(2)}) copy-start(pred[4,32]{1,0:T(4,128)(4,1)} %copy-done.20) | copy-start | bytes 388
  15.1 47.6 %collective-permute-start = (f32[4,64,128]{1,2,0:T(8,128)S(1)}, f32[4,64,128]{1,2,0:T(8,128)}, u32[]{:S(2)}, u32[]{:S(2)}) collective-permute-start(f32[4,64,128]{1,2,0:T(8,128)S(1)} %bitcast.158), channel_id=1, source_target_pairs={{8,0},{12,4},{9,1},{13,5},{10,2},{14,6},{11,3},{15,7},{24,16},{28,... | collective-permute-start | bytes 393224 | tf_op jit(solution)/shard_map/ppermute | solution.py:20
  17.2 45.6 %collective-permute-start.1 = (f32[4,64,128]{1,2,0:T(8,128)}, f32[4,64,128]{1,2,0:T(8,128)}, u32[]{:S(2)}, u32[]{:S(2)}) collective-permute-start(f32[4,64,128]{1,2,0:T(8,128)} %bitcast.14), channel_id=1, source_target_pairs={{4,0},{8,4},{12,8},{5,1},{9,5},{13,9},{6,2},{10,6},{14,10},{7,3},{... | collective-permute-start | bytes 393224 | tf_op jit(solution)/shard_map/ppermute | solution.py:20
  19.2 43.6 %collective-permute-start.2 = (f32[4,64,128]{1,2,0:T(8,128)}, f32[4,64,128]{1,2,0:T(8,128)}, u32[]{:S(2)}, u32[]{:S(2)}) collective-permute-start(f32[4,64,128]{1,2,0:T(8,128)} %bitcast.16), channel_id=1, source_target_pairs={{0,4},{4,8},{8,12},{1,5},{5,9},{9,13},{2,6},{6,10},{10,14},{3,7},{... | collective-permute-start | bytes 393224 | tf_op jit(solution)/shard_map/ppermute | solution.py:20
  23.7 39.1 %collective-permute-start.3 = (f32[4,64,128]{1,2,0:T(8,128)}, f32[4,64,128]{1,2,0:T(8,128)}, u32[]{:S(2)}, u32[]{:S(2)}) collective-permute-start(f32[4,64,128]{1,2,0:T(8,128)} %bitcast.18), channel_id=1, source_target_pairs={{0,8},{4,12},{1,9},{5,13},{2,10},{6,14},{3,11},{7,15},{16,24},{20,... | collective-permute-start | bytes 393224 | tf_op jit(solution)/shard_map/ppermute | solution.py:20
  34.0 6.2 %copy-start.13 = (s32[4,4]{1,0:T(4,128)S(1)}, s32[4,4]{1,0:T(4,128)}, u32[]{:S(2)}) copy-start(s32[4,4]{1,0:T(4,128)} %select_reduce_fusion) | copy-start | bytes 196
  34.0 6.9 %copy-start.14 = (f32[1,4,4]{2,1,0:T(4,128)S(1)}, f32[1,4,4]{2,1,0:T(4,128)}, u32[]{:S(2)}) copy-start(f32[1,4,4]{2,1,0:T(4,128)} %get-tuple-element.55) | copy-start | bytes 196
  35.8 5.9 %copy-start.1 = (f32[32,64,64]{2,1,0:T(8,128)S(1)}, f32[32,64,64]{2,1,0:T(8,128)}, u32[]{:S(2)}) copy-start(f32[32,64,64]{2,1,0:T(8,128)} %copy.70) | copy-start | bytes 1572868
  47.1 6.2 %copy-start.19 = (pred[4,32]{1,0:T(4,128)(4,1)S(1)}, pred[4,32]{1,0:T(4,128)(4,1)}, u32[]{:S(2)}) copy-start(pred[4,32]{1,0:T(4,128)(4,1)} %copy-done.18) | copy-start | bytes 388
  68.2 11.1 %copy-start.17 = (pred[4,32]{1,0:T(4,128)(4,1)S(1)}, pred[4,32]{1,0:T(4,128)(4,1)}, u32[]{:S(2)}) copy-start(pred[4,32]{1,0:T(4,128)(4,1)} %copy-done.16) | copy-start | bytes 388
  70.1 14.7 %collective-permute-start.4 = (f32[1,64,128]{2,1,0:T(8,128)S(1)}, f32[1,64,128]{2,1,0:T(8,128)S(1)}, u32[]{:S(2)}, u32[]{:S(2)}) collective-permute-start(f32[1,64,128]{2,1,0:T(8,128)S(1)} %get-tuple-element.33), channel_id=1, source_target_pairs={{4,0},{8,4},{12,8},{5,1},{9,5},{13,9},{6,2},{10,6},{14,10},{7,3},{... | collective-permute-start | bytes 98312 | tf_op jit(solution)/shard_map/ppermute | solution.py:33
  71.4 13.4 %collective-permute-start.5 = (f32[1,64,128]{2,1,0:T(8,128)S(1)}, f32[1,64,128]{2,1,0:T(8,128)S(1)}, u32[]{:S(2)}, u32[]{:S(2)}) collective-permute-start(f32[1,64,128]{2,1,0:T(8,128)S(1)} %get-tuple-element.34), channel_id=1, source_target_pairs={{0,4},{4,8},{8,12},{1,5},{5,9},{9,13},{2,6},{6,10},{10,14},{3,7},{... | collective-permute-start | bytes 98312 | tf_op jit(solution)/shard_map/ppermute | solution.py:31
  74.4 9.8 %collective-permute-start.6 = (f32[32,1,128]{2,1,0:T(1,128)S(1)}, f32[32,1,128]{2,1,0:T(1,128)S(1)}, u32[]{:S(2)}, u32[]{:S(2)}) collective-permute-start(f32[32,1,128]{2,1,0:T(1,128)S(1)} %get-tuple-element.35), channel_id=1, source_target_pairs={{1,0},{2,1},{3,2},{0,3},{5,4},{6,5},{7,6},{4,7},{9,8},{10,9},{11,1... | collective-permute-start | bytes 49160 | tf_op jit(solution)/shard_map/ppermute | solution.py:33
  79.2 5.5 %collective-permute-start.7 = (f32[32,1,128]{2,1,0:T(1,128)S(1)}, f32[32,1,128]{2,1,0:T(1,128)S(1)}, u32[]{:S(2)}, u32[]{:S(2)}) collective-permute-start(f32[32,1,128]{2,1,0:T(1,128)S(1)} %get-tuple-element.36), channel_id=1, source_target_pairs={{0,1},{1,2},{2,3},{3,0},{4,5},{5,6},{6,7},{7,4},{8,9},{9,10},{10,1... | collective-permute-start | bytes 49160 | tf_op jit(solution)/shard_map/ppermute | solution.py:31
  140.6 12.0 %copy-start = (f32[32,64,64]{2,1,0:T(8,128)S(1)}, f32[32,64,64]{2,1,0:T(8,128)}, u32[]{:S(2)}) copy-start(f32[32,64,64]{2,1,0:T(8,128)} %copy.84) | copy-start | bytes 1572868
  140.7 26.8 %collective-permute-start.8 = (f32[4,64,128]{1,2,0:T(8,128)S(1)}, f32[4,64,128]{1,2,0:T(8,128)S(1)}, u32[]{:S(2)}, u32[]{:S(2)}) collective-permute-start(f32[4,64,128]{1,2,0:T(8,128)S(1)} %bitcast.159), channel_id=1, source_target_pairs={{8,0},{12,4},{9,1},{13,5},{10,2},{14,6},{11,3},{15,7},{24,16},{28,... | collective-permute-start | bytes 393224 | tf_op jit(solution)/shard_map/ppermute | solution.py:20
  142.2 25.3 %collective-permute-start.9 = (f32[4,64,128]{1,2,0:T(8,128)S(1)}, f32[4,64,128]{1,2,0:T(8,128)}, u32[]{:S(2)}, u32[]{:S(2)}) collective-permute-start(f32[4,64,128]{1,2,0:T(8,128)S(1)} %bitcast.160), channel_id=1, source_target_pairs={{4,0},{8,4},{12,8},{5,1},{9,5},{13,9},{6,2},{10,6},{14,10},{7,3},{... | collective-permute-start | bytes 393224 | tf_op jit(solution)/shard_map/ppermute | solution.py:20
  143.5 24.0 %collective-permute-start.10 = (f32[4,64,128]{1,2,0:T(8,128)S(1)}, f32[4,64,128]{1,2,0:T(8,128)}, u32[]{:S(2)}, u32[]{:S(2)}) collective-permute-start(f32[4,64,128]{1,2,0:T(8,128)S(1)} %bitcast.161), channel_id=1, source_target_pairs={{0,4},{4,8},{8,12},{1,5},{5,9},{9,13},{2,6},{6,10},{10,14},{3,7},{... | collective-permute-start | bytes 393224 | tf_op jit(solution)/shard_map/ppermute | solution.py:20
  147.3 8.8 %copy-start.27 = (f32[32]{0:T(128)S(1)}, f32[32]{0:T(128)}, u32[]{:S(2)}) copy-start(f32[32]{0:T(128)} %get-tuple-element.7) | copy-start | bytes 388
  147.3 8.8 %copy-start.29 = (f32[32]{0:T(128)S(1)}, f32[32]{0:T(128)}, u32[]{:S(2)}) copy-start(f32[32]{0:T(128)} %get-tuple-element.81) | copy-start | bytes 388
  147.3 8.8 %copy-start.30 = (f32[32]{0:T(128)S(1)}, f32[32]{0:T(128)}, u32[]{:S(2)}) copy-start(f32[32]{0:T(128)} %get-tuple-element.82) | copy-start | bytes 388
  147.3 8.8 %copy-start.31 = (f32[32]{0:T(128)S(1)}, f32[32]{0:T(128)}, u32[]{:S(2)}) copy-start(f32[32]{0:T(128)} %get-tuple-element.83) | copy-start | bytes 388
  147.3 20.2 %collective-permute-start.11 = (f32[4,64,128]{1,2,0:T(8,128)S(1)}, f32[4,64,128]{1,2,0:T(8,128)}, u32[]{:S(2)}, u32[]{:S(2)}) collective-permute-start(f32[4,64,128]{1,2,0:T(8,128)S(1)} %bitcast.162), channel_id=1, source_target_pairs={{0,8},{4,12},{1,9},{5,13},{2,10},{6,14},{3,11},{7,15},{16,24},{20,... | collective-permute-start | bytes 393224 | tf_op jit(solution)/shard_map/ppermute | solution.py:20
  170.0 11.2 %collective-permute-start.12 = (f32[1,64,128]{2,1,0:T(8,128)S(1)}, f32[1,64,128]{2,1,0:T(8,128)S(1)}, u32[]{:S(2)}, u32[]{:S(2)}) collective-permute-start(f32[1,64,128]{2,1,0:T(8,128)S(1)} %get-tuple-element.25), channel_id=1, source_target_pairs={{4,0},{8,4},{12,8},{5,1},{9,5},{13,9},{6,2},{10,6},{14,10},{7,3},{... | collective-permute-start | bytes 98312 | tf_op jit(solution)/shard_map/ppermute | solution.py:33
  171.3 9.9 %collective-permute-start.13 = (f32[1,64,128]{2,1,0:T(8,128)S(1)}, f32[1,64,128]{2,1,0:T(8,128)S(1)}, u32[]{:S(2)}, u32[]{:S(2)}) collective-permute-start(f32[1,64,128]{2,1,0:T(8,128)S(1)} %get-tuple-element.26), channel_id=1, source_target_pairs={{0,4},{4,8},{8,12},{1,5},{5,9},{9,13},{2,6},{6,10},{10,14},{3,7},{... | collective-permute-start | bytes 98312 | tf_op jit(solution)/shard_map/ppermute | solution.py:31
  174.4 4.0 %collective-permute-start.14 = (f32[32,1,128]{2,1,0:T(1,128)S(1)}, f32[32,1,128]{2,1,0:T(1,128)S(1)}, u32[]{:S(2)}, u32[]{:S(2)}) collective-permute-start(f32[32,1,128]{2,1,0:T(1,128)S(1)} %get-tuple-element.27), channel_id=1, source_target_pairs={{1,0},{2,1},{3,2},{0,3},{5,4},{6,5},{7,6},{4,7},{9,8},{10,9},{11,1... | collective-permute-start | bytes 49160 | tf_op jit(solution)/shard_map/ppermute | solution.py:33
  175.7 5.5 %collective-permute-start.15 = (f32[32,1,128]{2,1,0:T(1,128)S(1)}, f32[32,1,128]{2,1,0:T(1,128)S(1)}, u32[]{:S(2)}, u32[]{:S(2)}) collective-permute-start(f32[32,1,128]{2,1,0:T(1,128)S(1)} %get-tuple-element.28), channel_id=1, source_target_pairs={{0,1},{1,2},{2,3},{3,0},{4,5},{5,6},{6,7},{7,4},{8,9},{9,10},{10,1... | collective-permute-start | bytes 49160 | tf_op jit(solution)/shard_map/ppermute | solution.py:31
  (16 other events, 35.6 us)
